TPU v7x, 512 devices: a whole 4x8x8 slice. The times are simulated.
512 devices in a mesh: sub: 8 (over x, core), seq: 8 (over y), exp: 8 (over z).
Axes of the slice: x: 4, y: 8, z: 8, core: 2. Of those that a mesh axis runs over, the one named last changes fastest.
Arguments:
- node_features: bfloat16 [64, 1536, 1024], P(('sub', 'exp'), 'seq'), parts along dimension 0, may hold values from -24 to 24
- block_mask: int32 [64, 12, 12], P(('sub', 'exp')), parts along dimension 0, may hold values from 0 to 1, as said below
- w_qkv: bfloat16 [1024, 3072], P('exp', 'seq'), may hold values from -4 to 4
- w_out: bfloat16 [1024, 1024], P('seq', 'exp'), may hold values from -0.1875 to 0.1875
- norm_gain: float32 [1024], replicated, may hold values from 0.5 to 1.5
- routes: int32 [64, 1536, 2], P(('sub', 'exp'), 'seq'), parts along dimension 0, may hold values from 0 to 63, all different within a row; in each aligned block of 192 rows (0 to 191, 192 to 383, ..., all dimensions but the last counted through in order) at most 12 rows name the same one
- gates: float32 [64, 1536, 2], P(('sub', 'exp'), 'seq'), parts along dimension 0, may hold values from 0.1 to 1
- w_gate_up: bfloat16 [64, 1024, 1024], P(('seq', 'exp')), may hold values from -0.1875 to 0.1875
- w_down: bfloat16 [64, 512, 1024], P(('seq', 'exp')), may hold values from -0.25 to 0.25
Outputs:
- layer_out: bfloat16 [64, 1536, 1024], P(('sub', 'exp'), 'seq'), parts along dimension 0
There are 8 independent parts, one for each index of `sub`. A program takes and returns all parts, laid end to end along the dimension named above; an argument that names none is the same for every part. Nothing has to cross between parts.
Inputs may be any that keep to these rules, and one draw needn't show every extreme that they name: In each aligned block of 192 rows (one device's nodes, subgraphs then nodes in order) no expert is named by more than 12 of the rows' routes, a bound that some block reaches; the 2 experts of a node differ. `block_mask`: the diagonal blocks are 1.
All inputs are finite; a program needn't handle non-finite values.
Results may differ from a plain program's by a relative error of at most 0.0065.
The roundings to bfloat16 on the way count: a program that leaves them out, or rounds other values in their place, can miss the bound.
Values may be sent and summed in bfloat16 or wider, within the bound.
No kernel may reach another device: no remote copies, remote signals or barrier semaphores. Data moves between devices by JAX's collectives and lax.ppermute only.
A program may use at most 64 MiB of HBM per device.

v0:
```python
import math
import jax
import jax.numpy as jnp
from jax import lax
from jax.sharding import PartitionSpec as P

HEAD_DIM = 64
TOP = 2
BLOCK = 128


def per_device(
    node_features, block_mask, w_qkv, w_out, norm_gain, routes, gates, w_gate_up, w_down
):
    feats = node_features[0]
    node_dev, width = feats.shape
    seq_count = lax.axis_size("seq")
    exp_count = lax.axis_size("exp")
    experts = seq_count * exp_count * w_gate_up.shape[0]
    head_cols = w_qkv.shape[1]
    qkv_all, out_all = (
        lax.all_gather(w_qkv[None], ("seq", "exp"), axis=0, tiled=True),
        lax.all_gather(w_out[None], ("seq", "exp"), axis=0, tiled=True),
    )
    qkv_tiles = qkv_all.reshape(seq_count, exp_count, w_qkv.shape[0], head_cols)
    local_proj = jnp.einsum(
        "nek,sekc->nsc",
        feats.reshape(node_dev, exp_count, w_qkv.shape[0]),
        qkv_tiles,
        preferred_element_type=jnp.float32,
    )
    local_proj = local_proj.astype(jnp.bfloat16).reshape(node_dev, seq_count * head_cols)
    projected = lax.all_to_all(local_proj, "seq", split_axis=1, concat_axis=0, tiled=True)
    nodes = projected.shape[0]
    heads_here = head_cols // (3 * HEAD_DIM)
    split = projected.reshape(nodes, heads_here, 3, HEAD_DIM)
    query = split[:, :, 0]
    keys = split[:, :, 1]
    values = split[:, :, 2]
    col_mask = jnp.repeat(block_mask[0], BLOCK, axis=1) > 0
    span = math.gcd(nodes, 512)
    scale = 1.0 / math.sqrt(HEAD_DIM)

    def attend(index):
        start = index * span
        rows_query = lax.dynamic_slice_in_dim(query, start, span, 0)
        rows_mask = lax.dynamic_slice_in_dim(col_mask, start // BLOCK, span // BLOCK, 0)
        allowed = jnp.repeat(rows_mask, BLOCK, axis=0)
        scores = (
            jnp.einsum("qhd,khd->hqk", rows_query, keys, preferred_element_type=jnp.float32) * scale
        )
        scores = jnp.where(allowed[None], scores, -1e30)
        top = jnp.max(scores, axis=-1, keepdims=True)
        weights = jnp.exp(scores - top)
        probs = (weights / jnp.sum(weights, axis=-1, keepdims=True)).astype(jnp.bfloat16)
        return jnp.einsum("hqk,khd->qhd", probs, values, preferred_element_type=jnp.float32).astype(
            jnp.bfloat16
        )

    blocks = lax.map(attend, jnp.arange(nodes // span, dtype=jnp.int32))
    attended = blocks.reshape(nodes, heads_here * HEAD_DIM)
    node_attended = lax.all_to_all(attended, "seq", split_axis=0, concat_axis=1, tiled=True)
    out_tiles = out_all.reshape(seq_count, exp_count, w_out.shape[0], w_out.shape[1])
    attn_out = jnp.einsum(
        "nsk,sekc->nec",
        node_attended.reshape(node_dev, seq_count, w_out.shape[0]),
        out_tiles,
        preferred_element_type=jnp.float32,
    )
    mixed = feats.astype(jnp.float32) + attn_out.reshape(node_dev, width)
    mean_square = jnp.mean(mixed * mixed, axis=-1, keepdims=True)
    normed = (mixed * lax.rsqrt(mean_square + 1e-06) * norm_gain).astype(jnp.bfloat16)
    capacity = 2 * TOP * node_dev // experts
    pair_routes = routes[0].reshape(node_dev * TOP)
    onehot = (pair_routes[:, None] == jnp.arange(experts, dtype=jnp.int32)).astype(jnp.int32)
    earlier = jnp.cumsum(onehot, axis=0, dtype=jnp.int32) - onehot
    slots = jnp.sum(earlier * onehot, axis=1, dtype=jnp.int32)
    position = pair_routes * capacity + slots
    outgoing = (
        jnp.zeros((experts * capacity, width), jnp.bfloat16)
        .at[position]
        .set(jnp.repeat(normed, TOP, axis=0))
    )
    outgoing = outgoing.reshape(experts, capacity, width)
    hidden_units = w_down.shape[1]
    received = lax.all_to_all(outgoing, ("seq", "exp"), split_axis=0, concat_axis=0, tiled=True)
    sources, items, columns = received.shape
    flat_rows = received.reshape(sources * items, columns)
    both = jnp.dot(flat_rows, w_gate_up[0], preferred_element_type=jnp.float32)
    hidden = (jax.nn.silu(both[:, :hidden_units]) * both[:, hidden_units:]).astype(jnp.bfloat16)
    result = jnp.dot(hidden, w_down[0], preferred_element_type=jnp.float32).astype(jnp.bfloat16)
    processed = result.reshape(sources, items, columns)
    returned = lax.all_to_all(
        processed, ("seq", "exp"), split_axis=0, concat_axis=0, tiled=True
    ).reshape(experts * capacity, width)
    picked = returned[position].astype(jnp.float32).reshape(node_dev, TOP, width)
    expert_sum = jnp.sum(picked * gates[0][:, :, None], axis=1)
    return (mixed + expert_sum).astype(jnp.bfloat16)[None]


def solution(mesh):
    in_specs = (
        P(("sub", "exp"), "seq", None),
        P(("sub", "exp"), None, None),
        P("exp", "seq"),
        P("seq", "exp"),
        P(),
        P(("sub", "exp"), "seq", None),
        P(("sub", "exp"), "seq", None),
        P(("seq", "exp"), None, None),
        P(("seq", "exp"), None, None),
    )
    out_specs = P(("sub", "exp"), "seq", None)
    return jax.shard_map(
        per_device, mesh=mesh, in_specs=in_specs, out_specs=out_specs, check_vma=False
    )
```

profile of v0, /device:TPU:24, one launch (start us, length us, event | category | flops | bytes accessed | tf_op | source)
XLA Modules:
  0.0 382.8 jit_solution(14159090257780799350)
XLA Ops:
  8.3 97.1 %all-gather.5.cloned.1.call-done = bf16[8192,384]{1,0:T(8,128)(2,1)} async-done(((bf16[128,384]{1,0:T(8,128)(2,1)}), bf16[8192,384]{1,0:T(8,128)(2,1)}) %all-gather.5.cloned.1.call-update) | async-done | bytes 6291472 | tf_op jit(solution)/shard_map/all_gather | solution.py:22
  105.4 5.2 %bitcast_convert_fusion = bf16[192,8,384]{2,0,1:T(8,128)(2,1)} fusion(bf16[8,8,128,384]{3,2,1,0:T(8,128)(2,1)} %bitcast.99, bf16[192,8,128]{2,1,0:T(8,128)(2,1)S(1)} %bitcast.103), kind=kOutput, calls=%fused_computation.28 | convolution fusion | flops 1208549376 | bytes 7864320 | tf_op jit(solution)/shard_map/nek,sekc->nsc/dot_general | solution.py:26
  110.7 6.1 %all-to-all-start = ((bf16[192,8,384]{2,0,1:T(8,128)(2,1)}), bf16[192,8,384]{2,0,1:T(8,128)(2,1)S(1)}, u32[]{:S(2)}, u32[]{:S(2)}) async-start(bf16[192,8,384]{2,0,1:T(8,128)(2,1)} %bitcast_convert_fusion), calls=%async_computation | async-start | bytes 2359296 | tf_op jit(solution)/shard_map/all_to_all | solution.py:33
  118.1 26.0 %all-to-all-done = bf16[192,8,384]{2,0,1:T(8,128)(2,1)S(1)} async-done(((bf16[192,8,384]{2,0,1:T(8,128)(2,1)}), bf16[192,8,384]{2,0,1:T(8,128)(2,1)S(1)}, u32[]{:S(2)}, u32[]{:S(2)}) %all-to-all-start) | async-done | bytes 1179680 | tf_op jit(solution)/shard_map/all_to_all | solution.py:33
  150.1 28.0 %while.12 = (s32[]{:T(128)}, bf16[3,512,2,64]{1,3,2,0:T(8,128)(2,1)}, s32[3]{0:T(128)S(1)}, pred[12,1536]{1,0:T(8,128)(4,1)S(1)}, bf16[1536,2,64]{0,2,1:T(8,128)...) while((s32[]{:T(128)}, ...), condition=%wide.region_3.4_spmd, body=%wide.region_0.3_spmd.sunk | while | flops 618205184 | bytes 5532574 | solution.py:60
  151.5 3.5 fusion.73
  155.0 4.4 %fusion.74 = bf16[3,512,2,64]{1,3,2,0:T(8,128)(2,1)} fusion(bf16[3,512,2,64]{1,3,2,0:T(8,128)(2,1)} %get-tuple-element.174, s32[]{:T(128)} %get-tuple-element.173, bf16[1536,2,64]{0,2,1:T(8,128)(2,1)S(1)} %copy-done.3, f32[2,512]{1,0:T(2,128)S(1)} %fusion.73, pred[512,1536]{1,0:T(8,128)(4,1)S(1)} %bitcast.97, ...), kind=kOutput, calls=%fused_computation.13.clone.1 | convolution fusion | flops 410585600 | bytes 1839620 | tf_op jit(solution)/shard_map/while/body/eval_jaxpr/hqk,khd->qhd/dot_general | solution.py:56
  160.9 3.5 fusion.73
  164.4 4.4 %fusion.74 = bf16[3,512,2,64]{1,3,2,0:T(8,128)(2,1)} fusion(bf16[3,512,2,64]{1,3,2,0:T(8,128)(2,1)} %get-tuple-element.174, s32[]{:T(128)} %get-tuple-element.173, bf16[1536,2,64]{0,2,1:T(8,128)(2,1)S(1)} %copy-done.3, f32[2,512]{1,0:T(2,128)S(1)} %fusion.73, pred[512,1536]{1,0:T(8,128)(4,1)S(1)} %bitcast.97, ...), kind=kOutput, calls=%fused_computation.13.clone.1 | convolution fusion | flops 410585600 | bytes 1839620 | tf_op jit(solution)/shard_map/while/body/eval_jaxpr/hqk,khd->qhd/dot_general | solution.py:56
  170.2 3.5 fusion.73
  173.7 4.4 %fusion.74 = bf16[3,512,2,64]{1,3,2,0:T(8,128)(2,1)} fusion(bf16[3,512,2,64]{1,3,2,0:T(8,128)(2,1)} %get-tuple-element.174, s32[]{:T(128)} %get-tuple-element.173, bf16[1536,2,64]{0,2,1:T(8,128)(2,1)S(1)} %copy-done.3, f32[2,512]{1,0:T(2,128)S(1)} %fusion.73, pred[512,1536]{1,0:T(8,128)(4,1)S(1)} %bitcast.97, ...), kind=kOutput, calls=%fused_computation.13.clone.1 | convolution fusion | flops 410585600 | bytes 1839620 | tf_op jit(solution)/shard_map/while/body/eval_jaxpr/hqk,khd->qhd/dot_general | solution.py:56
  181.4 8.0 %all-to-all-start.1 = ((bf16[8,192,128]{2,1,0:T(8,128)(2,1)}), bf16[8,192,128]{2,1,0:T(8,128)(2,1)S(1)}, u32[]{:S(2)}, u32[]{:S(2)}) async-start(bf16[8,192,128]{2,1,0:T(8,128)(2,1)} %reshape.145), calls=%async_computation.1 | async-start | bytes 786432 | tf_op jit(solution)/shard_map/all_to_all | solution.py:62
  191.0 16.6 %all-gather.7.cloned.1.call-done = bf16[8192,128]{1,0:T(8,128)(2,1)} async-done(((bf16[128,128]{1,0:T(8,128)(2,1)}), bf16[8192,128]{1,0:T(8,128)(2,1)}) %all-gather.7.cloned.1.call-update) | async-done | bytes 2097168 | tf_op jit(solution)/shard_map/all_gather | solution.py:23
  207.6 4.0 %copy.21 = bf16[8,8,128,128]{2,3,1,0:T(8,128)(2,1)} copy(bf16[8,8,128,128]{3,2,1,0:T(8,128)(2,1)} %bitcast.101) | data formatting | bytes 4194304 | tf_op jit(solution)/shard_map/reshape | solution.py:63
  219.4 4.0 %scatter_custom_fusion = bf16[768,1024]{1,0:T(8,128)(2,1)} fusion(s32[384]{0:T(512)S(1)} %fusion.50, bf16[384,1024]{1,0:T(8,128)(2,1)} %reshape.134, bf16[]{:T(256)} %constant.96.clone.1), kind=kCustom, calls=%fused_computation.42 | custom fusion | bytes 1573376 | tf_op jit(solution)/shard_map/scatter | solution.py:82
  223.4 3.6 reshape.116
  227.0 59.8 %all_to_all.39 = bf16[64,12,1024]{2,1,0:T(8,128)(2,1)} all-to-all(bf16[64,12,1024]{2,1,0:T(8,128)(2,1)} %reshape.116), channel_id=1, replica_groups=mesh['sub'=8,'seq'=8,'exp'=8] {'seq','exp'}, dimensions={0} | all-to-all | bytes 3145728 | tf_op jit(solution)/shard_map/all_to_all | solution.py:86
  286.8 3.6 reshape.117
  295.9 3.6 reshape.118
  299.5 7.7 %all-to-all-start.3 = ((bf16[64,12,1024]{2,1,0:T(8,128)(2,1)}), bf16[64,12,1024]{2,1,0:T(8,128)(2,1)}, u32[]{:S(2)}, u32[]{:S(2)}) async-start(bf16[64,12,1024]{2,1,0:T(8,128)(2,1)} %reshape.118), calls=%async_computation.3 | async-start | bytes 4194304 | tf_op jit(solution)/shard_map/all_to_all | solution.py:93
  307.3 52.9 %all-to-all-done.3 = bf16[64,12,1024]{2,1,0:T(8,128)(2,1)} async-done(((bf16[64,12,1024]{2,1,0:T(8,128)(2,1)}), bf16[64,12,1024]{2,1,0:T(8,128)(2,1)}, u32[]{:S(2)}, u32[]{:S(2)}) %all-to-all-start.3) | async-done | bytes 1572896 | tf_op jit(solution)/shard_map/all_to_all | solution.py:93
  360.2 3.6 reshape.119
  363.8 5.0 %gather_fusion = bf16[384,1024]{1,0:T(8,128)(2,1)} fusion(bf16[768,1024]{1,0:T(8,128)(2,1)} %reshape.119, s32[1024]{0:T(1024)S(1)} %pad_clamp_fusion), kind=kCustom, calls=%fused_computation | custom fusion | bytes 1574400 | tf_op jit(solution)/shard_map/gather | solution.py:96
  371.7 3.4 multiply_reduce_fusion
  (72 shorter events, 33.5 us)
Async XLA Ops:
  6.5 283.9 %copy-start = (bf16[1,1024,1024]{2,1,0:T(8,128)(2,1)S(1)}, bf16[1,1024,1024]{2,1,0:T(8,128)(2,1)}, u32[]{:S(2)}) copy-start(bf16[1,1024,1024]{2,1,0:T(8,128)(2,1)} %param.18) | copy-start | bytes 6291460
  6.5 98.9 %all-gather.5.cloned.1.call-start = ((), (), s32[]{:S(2)}) async-start(), calls=%async_computation.4 | async-start | bytes 6389760 | tf_op jit(solution)/shard_map/all_gather | solution.py:22
  110.7 6.8 %copy-start.4 = (s32[1,192,2]{1,2,0:T(2,128)S(1)}, s32[1,192,2]{1,2,0:T(2,128)}, u32[]{:S(2)}) copy-start(s32[1,192,2]{1,2,0:T(2,128)} %param.16) | copy-start | bytes 4612
  110.7 7.2 %copy-start.5 = (s32[1,12,12]{2,0,1:T(1,128)S(1)}, s32[1,12,12]{2,0,1:T(1,128)}, u32[]{:S(2)}) copy-start(s32[1,12,12]{2,0,1:T(1,128)} %param.12) | copy-start | bytes 1732
  110.7 33.4 %all-to-all-start = ((bf16[192,8,384]{2,0,1:T(8,128)(2,1)}), bf16[192,8,384]{2,0,1:T(8,128)(2,1)S(1)}, u32[]{:S(2)}, u32[]{:S(2)}) async-start(bf16[192,8,384]{2,0,1:T(8,128)(2,1)} %bitcast_convert_fusion), calls=%async_computation | async-start | bytes 2359296 | tf_op jit(solution)/shard_map/all_to_all | solution.py:33
  116.7 90.9 %all-gather.7.cloned.1.call-start = ((), (), s32[]{:S(2)}) async-start(), calls=%async_computation.5 | async-start | bytes 2129920 | tf_op jit(solution)/shard_map/all_gather | solution.py:23
  151.5 3.5 copy-start.3
  160.9 3.5 copy-start.3
  170.2 3.5 copy-start.3
  181.4 30.2 %all-to-all-start.1 = ((bf16[8,192,128]{2,1,0:T(8,128)(2,1)}), bf16[8,192,128]{2,1,0:T(8,128)(2,1)S(1)}, u32[]{:S(2)}, u32[]{:S(2)}) async-start(bf16[8,192,128]{2,1,0:T(8,128)(2,1)} %reshape.145), calls=%async_computation.1 | async-start | bytes 786432 | tf_op jit(solution)/shard_map/all_to_all | solution.py:62
  207.6 4.7 %copy-start.1 = (bf16[1,192,1024]{2,1,0:T(8,128)(2,1)S(1)}, bf16[1,192,1024]{2,1,0:T(8,128)(2,1)}, u32[]{:S(2)}) copy-start(bf16[1,192,1024]{2,1,0:T(8,128)(2,1)} %param.11) | copy-start | bytes 1179652
  211.6 3.4 copy-start.6
  211.6 0.7 copy-start.2
  290.4 3.3 copy-start.8
  299.5 7.7 %copy-start.7 = (f32[1,192,2]{1,2,0:T(2,128)S(1)}, f32[1,192,2]{1,2,0:T(2,128)}, u32[]{:S(2)}) copy-start(f32[1,192,2]{1,2,0:T(2,128)} %param.17) | copy-start | bytes 4612
  299.5 60.7 %all-to-all-start.3 = ((bf16[64,12,1024]{2,1,0:T(8,128)(2,1)}), bf16[64,12,1024]{2,1,0:T(8,128)(2,1)}, u32[]{:S(2)}, u32[]{:S(2)}) async-start(bf16[64,12,1024]{2,1,0:T(8,128)(2,1)} %reshape.118), calls=%async_computation.3 | async-start | bytes 4194304 | tf_op jit(solution)/shard_map/all_to_all | solution.py:93
Sparse Core Ops, SparseCore 0:
  10.4 94.9 all-gather.4
  120.6 86.9 all-gather.6
where the time goes:
time: 384 us; the launch traced here: 383 us
  waiting for transfers between devices  194 us (51%)
  blocking collectives  59.8 us (16%)
  local copies, waits for them, and re-layouts  49.3 us (13%)
  matrix products  37 us (10%)
  starting transfers between devices  21.8 us (6%)
  between operations  13.6 us (4%)
  other arithmetic  5.53 us (1%)
    all_gather x1, waiting for transfers between devices, per_device(): lax.all_gather(w_qkv[None], ('seq', 'exp'), axis=0, tiled=True)  97.1 us
    all_to_all x1, blocking collectives, per_device(): lax.all_to_all(outgoing, ('seq', 'exp'), split_axis=0, concat_axis=0, til...  59.8 us
    all_to_all x1, waiting for transfers between devices, per_device(): lax.all_to_all(processed, ('seq', 'exp'), split_axis=0, concat_axis=0, ti...  52.9 us
    all_to_all x1, waiting for transfers between devices, per_device(): lax.all_to_all(local_proj, 'seq', split_axis=1, concat_axis=0, tiled=True)  26 us
    all_gather x1, waiting for transfers between devices, per_device(): lax.all_gather(w_out[None], ('seq', 'exp'), axis=0, tiled=True)  16.6 us
    dot_general x3, matrix products, attend(): jnp.einsum('hqk,khd->qhd', probs, values, preferred_element_type=jnp.floa...  13.2 us
    sub x3, matrix products, attend(): weights = jnp.exp(scores - top)  10.4 us
    all_to_all x1, starting transfers between devices, per_device(): lax.all_to_all(attended, 'seq', split_axis=0, concat_axis=1, tiled=True)  8.03 us
  transfers between devices with their start and end apart: 5, of which 4 were waited for; matrix products, arithmetic and copies ran while one was open for 11% of the time, Pallas kernels for 0%

commit v1 on v0

--- a/solution.py
+++ b/solution.py
@@ -20,7 +20,12 @@
     head_cols = w_qkv.shape[1]
     qkv_all, out_all = (
         lax.all_gather(w_qkv[None], ("seq", "exp"), axis=0, tiled=True),
-        lax.all_gather(w_out[None], ("seq", "exp"), axis=0, tiled=True),
+        jnp.concatenate(
+            lax.all_to_all(
+                jnp.stack([w_out[None]] * lax.axis_size(("seq", "exp"))), ("seq", "exp"), 0, 0
+            ),
+            axis=0,
+        ),
     )
     qkv_tiles = qkv_all.reshape(seq_count, exp_count, w_qkv.shape[0], head_cols)
     local_proj = jnp.einsum(

time: 384 us -> 405 us (1.055)
  waiting for transfers between devices: 194 us -> 204 us
  starting transfers between devices: 21.8 us -> 29 us
  blocking collectives: 59.8 us -> 64.8 us
    all_to_all x0 -> x1, waiting for transfers between devices: none -> 19.6 us  [per_device(): lax.all_to_all(jnp.stack([w_out[None]] * lax.axis_size(('seq', 'exp'))),...]
    all_gather x1 -> x0, waiting for transfers between devices: 16.6 us -> none  [per_device(): lax.all_gather(w_out[None], ('seq', 'exp'), axis=0, tiled=True)]
    all_to_all x0 -> x1, starting transfers between devices: none -> 9.72 us  [per_device(): lax.all_to_all(jnp.stack([w_out[None]] * lax.axis_size(('seq', 'exp'))),...]
    all_to_all x1, waiting for transfers between devices: 0.01 us -> 7.18 us  [per_device(): lax.all_to_all(attended, 'seq', split_axis=0, concat_axis=1, tiled=True)]
    all_to_all x1, blocking collectives: 59.8 us -> 64.8 us  [per_device(): lax.all_to_all(outgoing, ('seq', 'exp'), split_axis=0, concat_axis=0, til...]
  transfers between devices with their start and end apart: 5 -> 5, of which waited for: 4 -> 5; matrix products, arithmetic and copies ran while one was open for 11% -> 10% of each run, Pallas kernels for 0% -> 0%
where the time goes in v1:
time: 405 us; the launch traced here: 403 us
  waiting for transfers between devices  204 us (50%)
  blocking collectives  64.8 us (16%)
  local copies, waits for them, and re-layouts  47.3 us (12%)
  matrix products  37 us (9%)
  starting transfers between devices  29 us (7%)
  between operations  13.6 us (3%)
  other arithmetic  5.53 us (1%)
    all_gather x1, waiting for transfers between devices, per_device(): lax.all_gather(w_qkv[None], ('seq', 'exp'), axis=0, tiled=True)  97.1 us
    all_to_all x1, blocking collectives, per_device(): lax.all_to_all(outgoing, ('seq', 'exp'), split_axis=0, concat_axis=0, til...  64.8 us
    all_to_all x1, waiting for transfers between devices, per_device(): lax.all_to_all(processed, ('seq', 'exp'), split_axis=0, concat_axis=0, ti...  52.5 us
    all_to_all x1, waiting for transfers between devices, per_device(): lax.all_to_all(local_proj, 'seq', split_axis=1, concat_axis=0, tiled=True)  27 us
    all_to_all x1, waiting for transfers between devices, per_device(): lax.all_to_all(jnp.stack([w_out[None]] * lax.axis_size(('seq', 'exp'))),...  19.6 us
    dot_general x3, matrix products, attend(): jnp.einsum('hqk,khd->qhd', probs, values, preferred_element_type=jnp.floa...  13.2 us
    sub x3, matrix products, attend(): weights = jnp.exp(scores - top)  10.4 us
    all_to_all x1, starting transfers between devices, per_device(): lax.all_to_all(jnp.stack([w_out[None]] * lax.axis_size(('seq', 'exp'))),...  9.72 us
  transfers between devices with their start and end apart: 5, of which 5 were waited for; matrix products, arithmetic and copies ran while one was open for 10% of the time, Pallas kernels for 0%

profile of v1, /device:TPU:24, one launch (start us, length us, event | category | flops | bytes accessed | tf_op | source)
XLA Modules:
  0.0 403.3 jit_solution(16632583228420357786)
XLA Ops:
  8.3 97.1 %all-gather.3.cloned.1.call-done = bf16[8192,384]{1,0:T(8,128)(2,1)} async-done(((bf16[128,384]{1,0:T(8,128)(2,1)}), bf16[8192,384]{1,0:T(8,128)(2,1)}) %all-gather.3.cloned.1.call-update) | async-done | bytes 6291472 | tf_op jit(solution)/shard_map/all_gather | solution.py:22
  105.4 5.2 %bitcast_convert_fusion = bf16[192,8,384]{2,0,1:T(8,128)(2,1)} fusion(bf16[8,8,128,384]{3,2,1,0:T(8,128)(2,1)} %bitcast.99, bf16[192,8,128]{2,1,0:T(8,128)(2,1)S(1)} %bitcast.102), kind=kOutput, calls=%fused_computation.28 | convolution fusion | flops 1208549376 | bytes 7864320 | tf_op jit(solution)/shard_map/nek,sekc->nsc/dot_general | solution.py:31
  110.7 6.1 %all-to-all-start = ((bf16[192,8,384]{2,0,1:T(8,128)(2,1)}), bf16[192,8,384]{2,0,1:T(8,128)(2,1)S(1)}, u32[]{:S(2)}, u32[]{:S(2)}) async-start(bf16[192,8,384]{2,0,1:T(8,128)(2,1)} %bitcast_convert_fusion), calls=%async_computation | async-start | bytes 2359296 | tf_op jit(solution)/shard_map/all_to_all | solution.py:38
  116.8 27.0 %all-to-all-done = bf16[192,8,384]{2,0,1:T(8,128)(2,1)S(1)} async-done(((bf16[192,8,384]{2,0,1:T(8,128)(2,1)}), bf16[192,8,384]{2,0,1:T(8,128)(2,1)S(1)}, u32[]{:S(2)}, u32[]{:S(2)}) %all-to-all-start) | async-done | bytes 1179680 | tf_op jit(solution)/shard_map/all_to_all | solution.py:38
  145.6 9.7 %all-to-all-start.2 = ((bf16[64,1,128,128]{2,3,1,0:T(8,128)(2,1)}), bf16[64,1,128,128]{2,3,1,0:T(8,128)(2,1)}, u32[]{:S(2)}, u32[]{:S(2)}) async-start(bf16[64,1,128,128]{2,3,1,0:T(8,128)(2,1)} %stack.3), calls=%async_computation.2 | async-start | bytes 4194304 | tf_op jit(solution)/shard_map/all_to_all | solution.py:24
  162.0 28.1 %while.12 = (s32[]{:T(128)}, bf16[3,512,2,64]{1,3,2,0:T(8,128)(2,1)}, s32[3]{0:T(128)S(1)}, pred[12,1536]{1,0:T(8,128)(4,1)S(1)}, bf16[1536,2,64]{0,2,1:T(8,128)...) while((s32[]{:T(128)}, ...), condition=%wide.region_3.4_spmd, body=%wide.region_0.3_spmd.sunk | while | flops 618205184 | bytes 5532574 | solution.py:65
  163.4 3.5 fusion.73
  166.9 4.4 %fusion.74 = bf16[3,512,2,64]{1,3,2,0:T(8,128)(2,1)} fusion(bf16[3,512,2,64]{1,3,2,0:T(8,128)(2,1)} %get-tuple-element.174, s32[]{:T(128)} %get-tuple-element.173, bf16[1536,2,64]{0,2,1:T(8,128)(2,1)S(1)} %copy-done.3, f32[2,512]{1,0:T(2,128)S(1)} %fusion.73, pred[512,1536]{1,0:T(8,128)(4,1)S(1)} %bitcast.98, ...), kind=kOutput, calls=%fused_computation.13.clone.1 | convolution fusion | flops 410585600 | bytes 1839620 | tf_op jit(solution)/shard_map/while/body/eval_jaxpr/hqk,khd->qhd/dot_general | solution.py:61
  172.8 3.5 fusion.73
  176.3 4.4 %fusion.74 = bf16[3,512,2,64]{1,3,2,0:T(8,128)(2,1)} fusion(bf16[3,512,2,64]{1,3,2,0:T(8,128)(2,1)} %get-tuple-element.174, s32[]{:T(128)} %get-tuple-element.173, bf16[1536,2,64]{0,2,1:T(8,128)(2,1)S(1)} %copy-done.3, f32[2,512]{1,0:T(2,128)S(1)} %fusion.73, pred[512,1536]{1,0:T(8,128)(4,1)S(1)} %bitcast.98, ...), kind=kOutput, calls=%fused_computation.13.clone.1 | convolution fusion | flops 410585600 | bytes 1839620 | tf_op jit(solution)/shard_map/while/body/eval_jaxpr/hqk,khd->qhd/dot_general | solution.py:61
  182.1 3.5 fusion.73
  185.6 4.4 %fusion.74 = bf16[3,512,2,64]{1,3,2,0:T(8,128)(2,1)} fusion(bf16[3,512,2,64]{1,3,2,0:T(8,128)(2,1)} %get-tuple-element.174, s32[]{:T(128)} %get-tuple-element.173, bf16[1536,2,64]{0,2,1:T(8,128)(2,1)S(1)} %copy-done.3, f32[2,512]{1,0:T(2,128)S(1)} %fusion.73, pred[512,1536]{1,0:T(8,128)(4,1)S(1)} %bitcast.98, ...), kind=kOutput, calls=%fused_computation.13.clone.1 | convolution fusion | flops 410585600 | bytes 1839620 | tf_op jit(solution)/shard_map/while/body/eval_jaxpr/hqk,khd->qhd/dot_general | solution.py:61
  193.4 19.6 %all-to-all-done.2 = bf16[64,1,128,128]{2,3,1,0:T(8,128)(2,1)} async-done(((bf16[64,1,128,128]{2,3,1,0:T(8,128)(2,1)}), bf16[64,1,128,128]{2,3,1,0:T(8,128)(2,1)}, u32[]{:S(2)}, u32[]{:S(2)}) %all-to-all-start.2) | async-done | bytes 2097184 | tf_op jit(solution)/shard_map/all_to_all | solution.py:24
  213.0 5.1 %all-to-all-start.1 = ((bf16[8,192,128]{2,1,0:T(8,128)(2,1)}), bf16[8,192,128]{2,1,0:T(8,128)(2,1)S(1)}, u32[]{:S(2)}, u32[]{:S(2)}) async-start(bf16[8,192,128]{2,1,0:T(8,128)(2,1)} %reshape.141), calls=%async_computation.1 | async-start | bytes 786432 | tf_op jit(solution)/shard_map/all_to_all | solution.py:67
  219.7 7.2 %all-to-all-done.1 = bf16[8,192,128]{2,1,0:T(8,128)(2,1)S(1)} async-done(((bf16[8,192,128]{2,1,0:T(8,128)(2,1)}), bf16[8,192,128]{2,1,0:T(8,128)(2,1)S(1)}, u32[]{:S(2)}, u32[]{:S(2)}) %all-to-all-start.1) | async-done | bytes 393248 | tf_op jit(solution)/shard_map/all_to_all | solution.py:67
  234.7 4.0 scatter_custom_fusion
  238.7 3.6 reshape.114
  242.3 64.8 %all_to_all.44 = bf16[64,12,1024]{2,1,0:T(8,128)(2,1)} all-to-all(bf16[64,12,1024]{2,1,0:T(8,128)(2,1)} %reshape.114), channel_id=1, replica_groups=mesh['sub'=8,'seq'=8,'exp'=8] {'seq','exp'}, dimensions={0} | all-to-all | bytes 3145728 | tf_op jit(solution)/shard_map/all_to_all | solution.py:91
  307.1 3.6 reshape.115
  316.2 3.6 reshape.116
  319.8 8.1 %all-to-all-start.4 = ((bf16[64,12,1024]{2,1,0:T(8,128)(2,1)}), bf16[64,12,1024]{2,1,0:T(8,128)(2,1)}, u32[]{:S(2)}, u32[]{:S(2)}) async-start(bf16[64,12,1024]{2,1,0:T(8,128)(2,1)} %reshape.116), calls=%async_computation.4 | async-start | bytes 4194304 | tf_op jit(solution)/shard_map/all_to_all | solution.py:98
  328.1 52.5 %all-to-all-done.4 = bf16[64,12,1024]{2,1,0:T(8,128)(2,1)} async-done(((bf16[64,12,1024]{2,1,0:T(8,128)(2,1)}), bf16[64,12,1024]{2,1,0:T(8,128)(2,1)}, u32[]{:S(2)}, u32[]{:S(2)}) %all-to-all-start.4) | async-done | bytes 1572896 | tf_op jit(solution)/shard_map/all_to_all | solution.py:98
  380.6 3.6 reshape.117
  384.2 5.0 %gather_fusion = bf16[384,1024]{1,0:T(8,128)(2,1)} fusion(bf16[768,1024]{1,0:T(8,128)(2,1)} %reshape.117, s32[1024]{0:T(1024)S(1)} %pad_clamp_fusion), kind=kCustom, calls=%fused_computation | custom fusion | bytes 1574400 | tf_op jit(solution)/shard_map/gather | solution.py:101
  (74 shorter events, 38.3 us)
Async XLA Ops:
  6.5 304.2 %copy-start = (bf16[1,1024,1024]{2,1,0:T(8,128)(2,1)S(1)}, bf16[1,1024,1024]{2,1,0:T(8,128)(2,1)}, u32[]{:S(2)}) copy-start(bf16[1,1024,1024]{2,1,0:T(8,128)(2,1)} %param.18) | copy-start | bytes 6291460
  6.5 98.9 %all-gather.3.cloned.1.call-start = ((), (), s32[]{:S(2)}) async-start(), calls=%async_computation.5 | async-start | bytes 6389760 | tf_op jit(solution)/shard_map/all_gather | solution.py:22
  110.7 6.1 %copy-start.4 = (bf16[128,128]{1,0:T(8,128)(2,1)S(1)}, bf16[128,128]{1,0:T(8,128)(2,1)}, u32[]{:S(2)}) copy-start(bf16[128,128]{1,0:T(8,128)(2,1)} %param.14) | copy-start | bytes 98308
  110.7 33.1 %all-to-all-start = ((bf16[192,8,384]{2,0,1:T(8,128)(2,1)}), bf16[192,8,384]{2,0,1:T(8,128)(2,1)S(1)}, u32[]{:S(2)}, u32[]{:S(2)}) async-start(bf16[192,8,384]{2,0,1:T(8,128)(2,1)} %bitcast_convert_fusion), calls=%async_computation | async-start | bytes 2359296 | tf_op jit(solution)/shard_map/all_to_all | solution.py:38
  145.6 9.7 %copy-start.5 = (s32[1,192,2]{1,2,0:T(2,128)S(1)}, s32[1,192,2]{1,2,0:T(2,128)}, u32[]{:S(2)}) copy-start(s32[1,192,2]{1,2,0:T(2,128)} %param.16) | copy-start | bytes 4612
  145.6 10.2 %copy-start.6 = (s32[1,12,12]{2,0,1:T(1,128)S(1)}, s32[1,12,12]{2,0,1:T(1,128)}, u32[]{:S(2)}) copy-start(s32[1,12,12]{2,0,1:T(1,128)} %param.12) | copy-start | bytes 1732
  145.6 67.4 %all-to-all-start.2 = ((bf16[64,1,128,128]{2,3,1,0:T(8,128)(2,1)}), bf16[64,1,128,128]{2,3,1,0:T(8,128)(2,1)}, u32[]{:S(2)}, u32[]{:S(2)}) async-start(bf16[64,1,128,128]{2,3,1,0:T(8,128)(2,1)} %stack.3), calls=%async_computation.2 | async-start | bytes 4194304 | tf_op jit(solution)/shard_map/all_to_all | solution.py:24
  163.4 3.5 copy-start.3
  172.8 3.5 copy-start.3
  182.1 3.5 copy-start.3
  190.0 37.6 %copy-start.1 = (bf16[1,192,1024]{2,1,0:T(8,128)(2,1)S(1)}, bf16[1,192,1024]{2,1,0:T(8,128)(2,1)}, u32[]{:S(2)}) copy-start(bf16[1,192,1024]{2,1,0:T(8,128)(2,1)} %param.11) | copy-start | bytes 1179652
  213.0 13.9 %all-to-all-start.1 = ((bf16[8,192,128]{2,1,0:T(8,128)(2,1)}), bf16[8,192,128]{2,1,0:T(8,128)(2,1)S(1)}, u32[]{:S(2)}, u32[]{:S(2)}) async-start(bf16[8,192,128]{2,1,0:T(8,128)(2,1)} %reshape.141), calls=%async_computation.1 | async-start | bytes 786432 | tf_op jit(solution)/shard_map/all_to_all | solution.py:67
  219.0 11.3 %copy-start.7 = (f32[1024]{0:T(1024)S(1)}, f32[1024]{0:T(1024)}, u32[]{:S(2)}) copy-start(f32[1024]{0:T(1024)} %param.15) | copy-start | bytes 12292
  226.9 0.7 copy-start.2
  310.8 3.3 copy-start.9
  319.8 8.2 %copy-start.8 = (f32[1,192,2]{1,2,0:T(2,128)S(1)}, f32[1,192,2]{1,2,0:T(2,128)}, u32[]{:S(2)}) copy-start(f32[1,192,2]{1,2,0:T(2,128)} %param.17) | copy-start | bytes 4612
  319.8 60.8 %all-to-all-start.4 = ((bf16[64,12,1024]{2,1,0:T(8,128)(2,1)}), bf16[64,12,1024]{2,1,0:T(8,128)(2,1)}, u32[]{:S(2)}, u32[]{:S(2)}) async-start(bf16[64,12,1024]{2,1,0:T(8,128)(2,1)} %reshape.116), calls=%async_computation.4 | async-start | bytes 4194304 | tf_op jit(solution)/shard_map/all_to_all | solution.py:98
Sparse Core Ops, SparseCore 0:
  10.4 94.9 all-gather.2
